TPU v7x, 32 devices: a whole 2x2x4 slice. The times are simulated.
32 devices in a mesh: dp: 4 (over z), pipe: 2 (over core), expert: 4 (over y, x).
Axes of the slice: x: 2, y: 2, z: 4, core: 2. Of those that a mesh axis runs over, the one named last changes fastest.
Arguments:
- tokens: bfloat16 [2, 96, 3072], P(None, 'expert'), may hold values from -6 to 6
- expert_ids: int32 [2, 2, 96, 2], P('pipe', None, 'expert'), may hold values from 0 to 3, all different within a row; in each aligned block of 24 rows (0 to 23, 24 to 47, ..., all dimensions but the last counted through in order) at most 16 rows name the same one
- gates: float32 [2, 2, 96, 2], P('pipe', None, 'expert'), may hold values from 0.1 to 1
- w_gate: bfloat16 [2, 4, 3072, 704], P('pipe', 'expert', None, 'dp'), may hold values from -0.109375 to 0.109375
- w_up: bfloat16 [2, 4, 3072, 704], P('pipe', 'expert', None, 'dp'), may hold values from -0.109375 to 0.109375
- w_down: bfloat16 [2, 4, 704, 3072], P('pipe', 'expert', 'dp'), may hold values from -0.3125 to 0.3125
Outputs:
- layer_out: bfloat16 [2, 2, 96, 3072], P('pipe', None, 'expert', 'dp')
Inputs may be any that keep to these rules, and one draw needn't show every extreme that they name: `expert_ids`: each token names 2 different experts in each layer. Among the tokens of one index of expert in one layer and micro-batch (aligned blocks of 24 tokens) no expert is named by more than 16 tokens, and in some block an expert is named by exactly 16.
All inputs are finite; a program needn't handle non-finite values.
Results may differ from a plain program's by a relative error of at most 0.0052.
Values may be sent and summed in bfloat16 or wider, within the bound.
No kernel may reach another device: no remote copies, remote signals or barrier semaphores. Data moves between devices by JAX's collectives and lax.ppermute only.
A program may use at most 64 MiB of HBM per device.

v0:
```python
import jax
import jax.numpy as jnp
from jax import lax
from jax.sharding import PartitionSpec as P

TOP = 2
CAP = 16
AXES = ("dp", "pipe", "expert")
SMALL_GROUP = 8


class Ring:

    def __init__(self, n):
        self.n = n
        self.xor = n & n - 1 == 0

    def ahead(self, me, s):
        return me ^ s if self.xor else (me + s) % self.n

    def behind(self, me, s):
        return me ^ s if self.xor else (me - s) % self.n

    def place(self, target, me):
        return target ^ me if self.xor else (target - me) % self.n


def build_maps(route_ids, route_gates, ring, me, rows_all):
    experts = ring.n
    flat_ids = route_ids.reshape(-1)
    onehot = (flat_ids[:, None] == jnp.arange(experts, dtype=jnp.int32)[None, :]).astype(jnp.int32)
    before = jnp.cumsum(onehot, axis=0) - onehot
    slot = jnp.sum(before * onehot, axis=1)
    placed = ring.place(flat_ids, me) * CAP + slot
    matches = jnp.arange(rows_all, dtype=jnp.int32)[:, None] == placed[None, :]
    dispatch_map = jnp.sum(matches.astype(jnp.float32).reshape(rows_all, -1, TOP), axis=2).astype(
        jnp.bfloat16
    )
    combine_map = jnp.sum(
        jnp.where(matches, route_gates.reshape(-1)[None, :], 0.0).reshape(rows_all, -1, TOP), axis=2
    )
    return (dispatch_map, combine_map)


def per_device(tokens, expert_ids, gates, w_gate, w_up, w_down):
    n_dp = lax.axis_size("dp")
    n_pipe = lax.axis_size("pipe")
    n_exp = lax.axis_size("expert")
    micro, tok_rows, width = tokens.shape
    units = w_gate.shape[3]
    columns = width // n_dp
    rows_all = n_exp * CAP
    d_me = lax.axis_index("dp")
    p_me = lax.axis_index("pipe")
    e_me = lax.axis_index("expert")
    dring = Ring(n_dp)
    ering = Ring(n_exp)
    small_dp = n_dp <= SMALL_GROUP

    def lin(d, p, e):
        return (d * n_pipe + p) * n_exp + e

    def expert_pairs(p, s, back):
        step = ering.behind if back else ering.ahead
        return [(lin(d, p, e), lin(d, p, step(e, s))) for d in range(n_dp) for e in range(n_exp)]

    def dp_pairs(p, s):
        return [
            (lin(d, p, e), lin(dring.ahead(d, s), p, e)) for d in range(n_dp) for e in range(n_exp)
        ]

    gate_local = w_gate[0, 0]
    up_local = w_up[0, 0]
    down_local = w_down[0, 0]
    if small_dp:
        down_parts = []
        for s in range(n_dp):
            piece = lax.dynamic_slice_in_dim(down_local, dring.ahead(d_me, s) * columns, columns, 1)
            down_parts.append(piece)
        down_parts, tokens = lax.optimization_barrier((down_parts, tokens))
        for s in range(1, n_dp):
            down_parts[s] = lax.ppermute(
                down_parts[s], "dp", [(i, dring.ahead(i, s)) for i in range(n_dp)]
            )
        down_full = jnp.concatenate(down_parts, axis=0)
    else:
        down_full = lax.all_to_all(down_local, "dp", 1, 0, tiled=True)
    route_ids = expert_ids[0]
    route_gates = gates[0]
    maps = [build_maps(route_ids[m], route_gates[m], ering, e_me, rows_all) for m in range(micro)]
    dispatch_map = jnp.stack([mp[0] for mp in maps])
    combine_map = jnp.stack([mp[1] for mp in maps])
    if ering.xor:
        combine_map = jnp.stack(
            [build_maps(route_ids[m], route_gates[m], ering, 0, rows_all)[1] for m in range(micro)]
        )

    def layer(current, p):
        outgoing = jnp.einsum(
            "mrt,mtd->mrd", dispatch_map, current, preferred_element_type=jnp.float32
        )
        outgoing = outgoing.astype(jnp.bfloat16).reshape(micro, n_exp, CAP, width)
        arrived = [outgoing[:, 0]]
        for s in range(1, n_exp):
            arrived.append(lax.ppermute(outgoing[:, s], AXES, expert_pairs(p, s, False)))
        flat_rows = jnp.stack(arrived, axis=1).reshape(-1, width)
        squares = jnp.mean(jnp.square(flat_rows.astype(jnp.float32)), axis=1, keepdims=True)
        inv_rms = lax.rsqrt(squares + 1e-05)
        gate_act = jnp.dot(flat_rows, gate_local, preferred_element_type=jnp.float32) * inv_rms
        up_act = jnp.dot(flat_rows, up_local, preferred_element_type=jnp.float32) * inv_rms
        hidden = (jax.nn.silu(gate_act) * up_act).astype(jnp.bfloat16)
        if small_dp:
            spread = jnp.broadcast_to(hidden[None], (n_dp,) + hidden.shape)
            gathered = lax.all_to_all(spread, "dp", 0, 0, tiled=True)
            order = jnp.stack([dring.behind(d_me, s) for s in range(n_dp)])
            gathered = jnp.take(gathered, order, axis=0)
            hidden_full = jnp.transpose(gathered, (1, 0, 2)).reshape(hidden.shape[0], n_dp * units)
        else:
            hidden_full = lax.all_gather(hidden, "dp", axis=1, tiled=True)
        expert_out = jnp.dot(hidden_full, down_full, preferred_element_type=jnp.float32).astype(
            jnp.bfloat16
        )
        expert_out = expert_out.reshape(micro, n_exp, CAP, columns)
        if ering.xor:
            order = jnp.stack([ering.place(j, e_me) for j in range(n_exp)])
            by_block = jnp.take(expert_out, order, axis=1)
            returned = lax.all_to_all(by_block, "expert", 1, 1, tiled=True).reshape(
                micro, rows_all, columns
            )
        else:
            returned = [expert_out[:, 0]]
            for s in range(1, n_exp):
                returned.append(lax.ppermute(expert_out[:, s], AXES, expert_pairs(p, s, True)))
            returned = jnp.stack(returned, axis=1).reshape(micro, rows_all, columns)
        mixed = jnp.einsum(
            "mrt,mrc->mtc",
            combine_map,
            returned.astype(jnp.float32),
            precision=lax.Precision.HIGHEST,
            preferred_element_type=jnp.float32,
        )
        current_cols = lax.dynamic_slice_in_dim(current, d_me * columns, columns, 2)
        return (current_cols.astype(jnp.float32) + mixed).astype(jnp.bfloat16)

    current = tokens
    result = None
    for p in range(n_pipe):
        cols = layer(current, p)
        result = cols if result is None else jnp.where(p_me == p, cols, result)
        if p + 1 < n_pipe:
            if small_dp:
                parts = []
                for s in range(n_dp):
                    pairs = [
                        (lin(d, p, e), lin(dring.ahead(d, s), p + 1, e))
                        for d in range(n_dp)
                        for e in range(n_exp)
                    ]
                    parts.append(lax.ppermute(cols, AXES, pairs))
                stacked = jnp.stack(parts)
                order = jnp.stack([dring.place(d_me, k) for k in range(n_dp)])
                stacked = jnp.take(stacked, order, axis=0)
                current = jnp.transpose(stacked, (1, 2, 0, 3)).reshape(micro, tok_rows, width)
            else:
                full = lax.all_gather(cols, "dp", axis=2, tiled=True)
                current = lax.ppermute(full, "pipe", [(p, p + 1)])
    return result[None]


def solution(mesh):
    return jax.shard_map(
        per_device,
        mesh=mesh,
        in_specs=(
            P(None, "expert", None),
            P("pipe", None, "expert", None),
            P("pipe", None, "expert", None),
            P("pipe", "expert", None, "dp"),
            P("pipe", "expert", None, "dp"),
            P("pipe", "expert", "dp", None),
        ),
        out_specs=P("pipe", None, "expert", "dp"),
        check_vma=False,
    )
```

profile of v0, /device:TPU:1, one launch (start us, length us, event | category | flops | bytes accessed | tf_op | source)
XLA Modules:
  0.0 94.3 jit_solution(11994145500577898993)
XLA Ops:
  0.0 2.2 %dynamic-slice_bitcast_fusion = (bf16[176,768]{1,0:T(8,128)(2,1)}, bf16[176,768]{1,0:T(8,128)(2,1)}, bf16[176,768]{1,0:T(8,128)(2,1)S(1)}, bf16[176,768]{1,0:T(8,128)(2,1)}) fusion(bf16[1,1,176,3072]{3,2,1,0:T(8,128)(2,1)} %param.15, s32[]{:T(128)S(6)} %select_n.72, s32[]{:T(128)S(6)} %select_n.70, s32[]{:T(128)S(6)} %select_n.69, s32[]{:T(128)S(6)} %select_n.71), kind=kLoop, calls=%fused_computation.33 | loop fusion | bytes 2162704 | tf_op jit(solution)/shard_map/dynamic_slice | solution.py:78
  2.2 2.1 %collective-permute-start.3 = (bf16[176,768]{1,0:T(8,128)(2,1)}, bf16[176,768]{1,0:T(8,128)(2,1)}, u32[]{:S(2)}, u32[]{:S(2)}) collective-permute-start(bf16[176,768]{1,0:T(8,128)(2,1)} %get-tuple-element.14), channel_id=1, source_target_pairs={{0,8},{8,0},{16,24},{24,16},{1,9},{9,1},{17,25},{25,17},{2,10},{10... | collective-permute-start | bytes 811016 | tf_op jit(solution)/shard_map/ppermute | solution.py:82
  4.4 2.3 %collective-permute-start.4 = (bf16[176,768]{1,0:T(8,128)(2,1)}, bf16[176,768]{1,0:T(8,128)(2,1)}, u32[]{:S(2)}, u32[]{:S(2)}) collective-permute-start(bf16[176,768]{1,0:T(8,128)(2,1)} %get-tuple-element.15), channel_id=1, source_target_pairs={{0,16},{8,24},{16,0},{24,8},{1,17},{9,25},{17,1},{25,9},{2,18},{10... | collective-permute-start | bytes 811016 | tf_op jit(solution)/shard_map/ppermute | solution.py:82
  6.7 0.1 copy.85
  6.8 0.1 eq.48
  7.0 0.2 select_reduce_fusion.3
  7.2 0.1 reduce_sum.85
  7.5 0.1 eq.55
  7.7 0.2 select_reduce_fusion.1
  7.9 0.1 reduce_sum.88
  8.1 0.1 convert_reduce_fusion
  8.2 0.4 convolution_convert_fusion.1
  8.7 0.7 fusion.20
  9.4 1.3 %collective-permute-start = (bf16[2,16,3072]{2,1,0:T(8,128)(2,1)}, bf16[2,16,3072]{2,1,0:T(8,128)(2,1)}, u32[]{:S(2)}, u32[]{:S(2)}) collective-permute-start(bf16[2,16,3072]{2,1,0:T(8,128)(2,1)} %get-tuple-element.35), channel_id=1, source_target_pairs={{0,1},{1,0},{2,3},{3,2},{8,9},{9,8},{10,11},{11,10},{16,17},{17,16... | collective-permute-start | bytes 589832 | tf_op jit(solution)/shard_map/ppermute | solution.py:105
  10.7 1.4 %collective-permute-start.1 = (bf16[2,16,3072]{2,1,0:T(8,128)(2,1)S(1)}, bf16[2,16,3072]{2,1,0:T(8,128)(2,1)}, u32[]{:S(2)}, u32[]{:S(2)}) collective-permute-start(bf16[2,16,3072]{2,1,0:T(8,128)(2,1)S(1)} %get-tuple-element.34), channel_id=1, source_target_pairs={{0,2},{1,3},{2,0},{3,1},{8,10},{9,11},{10,8},{11,9},{16,18},{17,19... | collective-permute-start | bytes 589832 | tf_op jit(solution)/shard_map/ppermute | solution.py:105
  12.1 1.3 %collective-permute-start.2 = (bf16[2,16,3072]{2,1,0:T(8,128)(2,1)S(1)}, bf16[2,16,3072]{2,1,0:T(8,128)(2,1)}, u32[]{:S(2)}, u32[]{:S(2)}) collective-permute-start(bf16[2,16,3072]{2,1,0:T(8,128)(2,1)S(1)} %get-tuple-element.36), channel_id=1, source_target_pairs={{0,3},{1,2},{2,1},{3,0},{8,11},{9,10},{10,9},{11,8},{16,19},{17,18... | collective-permute-start | bytes 589832 | tf_op jit(solution)/shard_map/ppermute | solution.py:105
  13.8 1.3 %multiply_reduce_fusion.1 = (f32[2,4,16]{2,1,0:T(4,128)S(1)}, bf16[2,4,16,3072]{3,2,1,0:T(8,128)(2,1)S(1)}) fusion(bf16[2,1,16,3072]{3,2,1,0:T(8,128)(2,1)} %bitcast.28, bf16[2,1,16,3072]{3,2,1,0:T(8,128)(2,1)} %bitcast.26, bf16[2,1,16,3072]{3,2,1,0:T(8,128)(2,1)} %bitcast.24, bf16[2,1,16,3072]{3,2,1,0:T(8,128)(2,1)S(1)} %get-tuple-element.33), kind=kLoop, calls=%fused_computation.8 | loop fusion | flops 2359168 | bytes 1573376 | tf_op jit(solution)/shard_map/reduce_sum | solution.py:107
  15.3 0.4 convolution_multiply_fusion.3
  15.7 0.8 copy-done.1
  16.5 0.5 fusion.6
  17.0 0.7 broadcast_in_dim.85
  17.7 4.5 %all-to-all-start = ((bf16[4,128,176]{1,2,0:T(8,128)(2,1)}), bf16[4,128,176]{1,2,0:T(8,128)(2,1)S(1)}, u32[]{:S(2)}, u32[]{:S(2)}) async-start(bf16[4,128,176]{1,2,0:T(8,128)(2,1)} %broadcast_in_dim.85), calls=%async_computation | async-start | bytes 360448 | tf_op jit(solution)/shard_map/all_to_all | solution.py:114
  22.2 1.0 %constant_dynamic-update-slice_fusion.2 = bf16[704,768]{1,0:T(8,128)(2,1)S(1)} fusion(bf16[704,768]{1,0:T(8,128)(2,1)S(1)} %constant_dynamic-update-slice_fusion.3, bf16[176,768]{1,0:T(8,128)(2,1)} %collective-permute-done.3), kind=kLoop, calls=%fused_computation.65 | loop fusion | bytes 540672
  23.2 1.0 %constant_dynamic-update-slice_fusion.1 = bf16[704,768]{1,0:T(8,128)(2,1)S(1)} fusion(bf16[704,768]{1,0:T(8,128)(2,1)S(1)} %constant_dynamic-update-slice_fusion.2, bf16[176,768]{1,0:T(8,128)(2,1)} %collective-permute-done.4), kind=kLoop, calls=%fused_computation.64 | loop fusion | bytes 540672
  24.1 1.0 %constant_dynamic-update-slice_fusion = bf16[704,768]{1,0:T(8,128)(2,1)S(1)} fusion(bf16[704,768]{1,0:T(8,128)(2,1)S(1)} %constant_dynamic-update-slice_fusion.1, bf16[176,768]{1,0:T(8,128)(2,1)} %collective-permute-done.5), kind=kLoop, calls=%fused_computation.63 | loop fusion | bytes 540672 | tf_op jit(solution)/shard_map/concatenate | solution.py:85
  25.1 7.9 %all-to-all-done = bf16[4,128,176]{1,2,0:T(8,128)(2,1)S(1)} async-done(((bf16[4,128,176]{1,2,0:T(8,128)(2,1)}), bf16[4,128,176]{1,2,0:T(8,128)(2,1)S(1)}, u32[]{:S(2)}, u32[]{:S(2)}) %all-to-all-start) | async-done | bytes 180256 | tf_op jit(solution)/shard_map/all_to_all | solution.py:114
  33.0 0.6 gather_fusion.1
  33.6 0.1 broadcast_select_fusion.1
  33.7 0.4 convolution_convert_fusion.3
  34.1 0.6 gather_fusion.2
  34.7 0.8 select_bitcast_fusion.2
  35.5 3.4 %all-to-all-start.1 = ((bf16[2,4,16,768]{3,2,0,1:T(8,128)(2,1)}), bf16[2,4,16,768]{3,2,0,1:T(8,128)(2,1)S(1)}, u32[]{:S(2)}, u32[]{:S(2)}) async-start(bf16[2,4,16,768]{3,2,0,1:T(8,128)(2,1)} %select_bitcast_fusion.2), calls=%async_computation.1 | async-start | bytes 393216 | tf_op jit(solution)/shard_map/all_to_all | solution.py:127
  39.0 0.1 select_reduce_fusion
  39.1 3.9 %all-to-all-done.1 = bf16[2,4,16,768]{3,2,0,1:T(8,128)(2,1)S(1)} async-done(((bf16[2,4,16,768]{3,2,0,1:T(8,128)(2,1)}), bf16[2,4,16,768]{3,2,0,1:T(8,128)(2,1)S(1)}, u32[]{:S(2)}, u32[]{:S(2)}) %all-to-all-start.1) | async-done | bytes 196640 | tf_op jit(solution)/shard_map/all_to_all | solution.py:127
  43.0 0.2 fusion
  43.2 1.3 %collective-permute-start.6 = (bf16[2,24,768]{2,1,0:T(8,128)(2,1)S(1)}, bf16[2,24,768]{2,1,0:T(8,128)(2,1)S(1)}, u32[]{:S(2)}, u32[]{:S(2)}) collective-permute-start(bf16[2,24,768]{2,1,0:T(8,128)(2,1)S(1)} %fusion), channel_id=1, source_target_pairs={{0,4},{1,5},{2,6},{3,7},{8,12},{9,13},{10,14},{11,15},{16,20},{17,... | collective-permute-start | bytes 221192 | tf_op jit(solution)/shard_map/ppermute | solution.py:159
  44.5 1.3 %collective-permute-start.7 = (bf16[2,24,768]{2,1,0:T(8,128)(2,1)S(1)}, bf16[2,24,768]{2,1,0:T(8,128)(2,1)S(1)}, u32[]{:S(2)}, u32[]{:S(2)}) collective-permute-start(bf16[2,24,768]{2,1,0:T(8,128)(2,1)S(1)} %fusion), channel_id=1, source_target_pairs={{0,12},{1,13},{2,14},{3,15},{8,4},{9,5},{10,6},{11,7},{16,28},{17,... | collective-permute-start | bytes 221192 | tf_op jit(solution)/shard_map/ppermute | solution.py:159
  45.8 1.3 %collective-permute-start.8 = (bf16[2,24,768]{2,1,0:T(8,128)(2,1)S(1)}, bf16[2,24,768]{2,1,0:T(8,128)(2,1)S(1)}, u32[]{:S(2)}, u32[]{:S(2)}) collective-permute-start(bf16[2,24,768]{2,1,0:T(8,128)(2,1)S(1)} %fusion), channel_id=1, source_target_pairs={{0,20},{1,21},{2,22},{3,23},{8,28},{9,29},{10,30},{11,31},{16,4},{... | collective-permute-start | bytes 221192 | tf_op jit(solution)/shard_map/ppermute | solution.py:159
  47.1 1.3 %collective-permute-start.9 = (bf16[2,24,768]{2,1,0:T(8,128)(2,1)S(1)}, bf16[2,24,768]{2,1,0:T(8,128)(2,1)S(1)}, u32[]{:S(2)}, u32[]{:S(2)}) collective-permute-start(bf16[2,24,768]{2,1,0:T(8,128)(2,1)S(1)} %fusion), channel_id=1, source_target_pairs={{0,28},{1,29},{2,30},{3,31},{8,20},{9,21},{10,22},{11,23},{16,12},... | collective-permute-start | bytes 221192 | tf_op jit(solution)/shard_map/ppermute | solution.py:159
  48.4 4.2 %collective-permute-done.6 = bf16[2,24,768]{2,1,0:T(8,128)(2,1)S(1)} collective-permute-done((bf16[2,24,768]{2,1,0:T(8,128)(2,1)S(1)}, bf16[2,24,768]{2,1,0:T(8,128)(2,1)S(1)}, u32[]{:S(2)}, u32[]{:S(2)}) %collective-permute-start.6) | collective-permute-done | bytes 73760 | tf_op jit(solution)/shard_map/ppermute | solution.py:159
  52.6 3.6 %collective-permute-done.7 = bf16[2,24,768]{2,1,0:T(8,128)(2,1)S(1)} collective-permute-done((bf16[2,24,768]{2,1,0:T(8,128)(2,1)S(1)}, bf16[2,24,768]{2,1,0:T(8,128)(2,1)S(1)}, u32[]{:S(2)}, u32[]{:S(2)}) %collective-permute-start.7) | collective-permute-done | bytes 73760 | tf_op jit(solution)/shard_map/ppermute | solution.py:159
  56.2 0.8 collective-permute-done.8
  57.0 2.3 %collective-permute-done.9 = bf16[2,24,768]{2,1,0:T(8,128)(2,1)S(1)} collective-permute-done((bf16[2,24,768]{2,1,0:T(8,128)(2,1)S(1)}, bf16[2,24,768]{2,1,0:T(8,128)(2,1)S(1)}, u32[]{:S(2)}, u32[]{:S(2)}) %collective-permute-start.9) | collective-permute-done | bytes 73760 | tf_op jit(solution)/shard_map/ppermute | solution.py:159
  59.4 0.6 gather_fusion
  60.0 0.1 select_bitcast_fusion
  60.1 0.4 convolution_convert_fusion
  60.6 2.7 %collective-permute-start.10 = (bf16[2,16,3072]{2,1,0:T(8,128)(2,1)S(1)}, bf16[2,16,3072]{2,1,0:T(8,128)(2,1)S(1)}, u32[]{:S(2)}, u32[]{:S(2)}) collective-permute-start(bf16[2,16,3072]{2,1,0:T(8,128)(2,1)S(1)} %get-tuple-element.31), channel_id=1, source_target_pairs={{4,5},{5,4},{6,7},{7,6},{12,13},{13,12},{14,15},{15,14},{20,21},{2... | collective-permute-start | bytes 589832 | tf_op jit(solution)/shard_map/ppermute | solution.py:105
  63.3 2.2 %collective-permute-start.11 = (bf16[2,16,3072]{2,1,0:T(8,128)(2,1)S(1)}, bf16[2,16,3072]{2,1,0:T(8,128)(2,1)S(1)}, u32[]{:S(2)}, u32[]{:S(2)}) collective-permute-start(bf16[2,16,3072]{2,1,0:T(8,128)(2,1)S(1)} %get-tuple-element.30), channel_id=1, source_target_pairs={{4,6},{5,7},{6,4},{7,5},{12,14},{13,15},{14,12},{15,13},{20,22},{2... | collective-permute-start | bytes 589832 | tf_op jit(solution)/shard_map/ppermute | solution.py:105
  65.5 3.5 %collective-permute-start.12 = (bf16[2,16,3072]{2,1,0:T(8,128)(2,1)S(1)}, bf16[2,16,3072]{2,1,0:T(8,128)(2,1)S(1)}, u32[]{:S(2)}, u32[]{:S(2)}) collective-permute-start(bf16[2,16,3072]{2,1,0:T(8,128)(2,1)S(1)} %get-tuple-element.32), channel_id=1, source_target_pairs={{4,7},{5,6},{6,5},{7,4},{12,15},{13,14},{14,13},{15,12},{20,23},{2... | collective-permute-start | bytes 589832 | tf_op jit(solution)/shard_map/ppermute | solution.py:105
  69.0 1.0 %collective-permute-done.11 = bf16[2,16,3072]{2,1,0:T(8,128)(2,1)S(1)} collective-permute-done((bf16[2,16,3072]{2,1,0:T(8,128)(2,1)S(1)}, bf16[2,16,3072]{2,1,0:T(8,128)(2,1)S(1)}, u32[]{:S(2)}, u32[]{:S(2)}) %collective-permute-start.11) | collective-permute-done | bytes 196640 | tf_op jit(solution)/shard_map/ppermute | solution.py:105
  70.0 2.9 %collective-permute-done.12 = bf16[2,16,3072]{2,1,0:T(8,128)(2,1)S(1)} collective-permute-done((bf16[2,16,3072]{2,1,0:T(8,128)(2,1)S(1)}, bf16[2,16,3072]{2,1,0:T(8,128)(2,1)S(1)}, u32[]{:S(2)}, u32[]{:S(2)}) %collective-permute-start.12) | collective-permute-done | bytes 196640 | tf_op jit(solution)/shard_map/ppermute | solution.py:105
  73.0 0.2 multiply_reduce_fusion
  73.2 0.1 rsqrt.25
  73.3 0.5 convolution_multiply_fusion.1
  73.8 0.8 copy-done.2
  74.6 0.5 fusion.7
  75.1 8.3 %all_to_all.20 = bf16[4,128,176]{1,2,0:T(8,128)(2,1)S(1)} all-to-all(bf16[4,128,176]{1,2,0:T(8,128)(2,1)S(1)} %broadcast_in_dim.87), channel_id=1, replica_groups=mesh['dp'=4,'pipe'=2,'expert'=4] {'dp'}, dimensions={0} | all-to-all | bytes 360448 | tf_op jit(solution)/shard_map/all_to_all | solution.py:114
  83.4 0.7 gather_fusion.3
  84.2 0.3 convolution_convert_fusion.2
  84.6 0.7 gather_fusion.4
  85.3 0.8 select_bitcast_fusion.1
  86.1 3.4 %all-to-all-start.3 = ((bf16[2,4,16,768]{3,2,0,1:T(8,128)(2,1)}), bf16[2,4,16,768]{3,2,0,1:T(8,128)(2,1)S(1)}, u32[]{:S(2)}, u32[]{:S(2)}) async-start(bf16[2,4,16,768]{3,2,0,1:T(8,128)(2,1)} %select_bitcast_fusion.1), calls=%async_computation.3 | async-start | bytes 393216 | tf_op jit(solution)/shard_map/all_to_all | solution.py:127
  89.4 4.0 %all-to-all-done.3 = bf16[2,4,16,768]{3,2,0,1:T(8,128)(2,1)S(1)} async-done(((bf16[2,4,16,768]{3,2,0,1:T(8,128)(2,1)}), bf16[2,4,16,768]{3,2,0,1:T(8,128)(2,1)S(1)}, u32[]{:S(2)}, u32[]{:S(2)}) %all-to-all-start.3) | async-done | bytes 196640 | tf_op jit(solution)/shard_map/all_to_all | solution.py:127
  93.5 0.9 fusion.5
  (59 shorter events, 1.4 us)
Async XLA Ops:
  0.0 15.3 %copy-start = (bf16[1,1,3072,176]{2,3,1,0:T(8,128)(2,1)S(1)}, bf16[1,1,3072,176]{2,3,1,0:T(8,128)(2,1)}, u32[]{:S(2)}) copy-start(bf16[1,1,3072,176]{2,3,1,0:T(8,128)(2,1)} %param.13) | copy-start | bytes 3244036
  0.0 6.7 %copy-start.4 = (s32[1,2,24,2]{2,3,1,0:T(2,128)S(1)}, s32[1,2,24,2]{2,3,1,0:T(2,128)}, u32[]{:S(2)}) copy-start(s32[1,2,24,2]{2,3,1,0:T(2,128)} %param.11) | copy-start | bytes 1156
  0.0 8.2 %copy-start.3 = (bf16[2,24,3072]{2,1,0:T(8,128)(2,1)S(1)}, bf16[2,24,3072]{2,1,0:T(8,128)(2,1)}, u32[]{:S(2)}) copy-start(bf16[2,24,3072]{2,1,0:T(8,128)(2,1)} %param.10) | copy-start | bytes 884740
  2.2 19.9 %collective-permute-start.3 = (bf16[176,768]{1,0:T(8,128)(2,1)}, bf16[176,768]{1,0:T(8,128)(2,1)}, u32[]{:S(2)}, u32[]{:S(2)}) collective-permute-start(bf16[176,768]{1,0:T(8,128)(2,1)} %get-tuple-element.14), channel_id=1, source_target_pairs={{0,8},{8,0},{16,24},{24,16},{1,9},{9,1},{17,25},{25,17},{2,10},{10... | collective-permute-start | bytes 811016 | tf_op jit(solution)/shard_map/ppermute | solution.py:82
  4.4 18.8 %collective-permute-start.4 = (bf16[176,768]{1,0:T(8,128)(2,1)}, bf16[176,768]{1,0:T(8,128)(2,1)}, u32[]{:S(2)}, u32[]{:S(2)}) collective-permute-start(bf16[176,768]{1,0:T(8,128)(2,1)} %get-tuple-element.15), channel_id=1, source_target_pairs={{0,16},{8,24},{16,0},{24,8},{1,17},{9,25},{17,1},{25,9},{2,18},{10... | collective-permute-start | bytes 811016 | tf_op jit(solution)/shard_map/ppermute | solution.py:82
  8.6 5.0 %copy-start.12 = (f32[1,2,24,2]{2,3,1,0:T(2,128)S(1)}, f32[1,2,24,2]{2,3,1,0:T(2,128)}, u32[]{:S(2)}) copy-start(f32[1,2,24,2]{2,3,1,0:T(2,128)} %param.12) | copy-start | bytes 1156
  9.4 4.3 %collective-permute-start = (bf16[2,16,3072]{2,1,0:T(8,128)(2,1)}, bf16[2,16,3072]{2,1,0:T(8,128)(2,1)}, u32[]{:S(2)}, u32[]{:S(2)}) collective-permute-start(bf16[2,16,3072]{2,1,0:T(8,128)(2,1)} %get-tuple-element.35), channel_id=1, source_target_pairs={{0,1},{1,0},{2,3},{3,2},{8,9},{9,8},{10,11},{11,10},{16,17},{17,16... | collective-permute-start | bytes 589832 | tf_op jit(solution)/shard_map/ppermute | solution.py:105
  10.7 3.0 %collective-permute-start.1 = (bf16[2,16,3072]{2,1,0:T(8,128)(2,1)S(1)}, bf16[2,16,3072]{2,1,0:T(8,128)(2,1)}, u32[]{:S(2)}, u32[]{:S(2)}) collective-permute-start(bf16[2,16,3072]{2,1,0:T(8,128)(2,1)S(1)} %get-tuple-element.34), channel_id=1, source_target_pairs={{0,2},{1,3},{2,0},{3,1},{8,10},{9,11},{10,8},{11,9},{16,18},{17,19... | collective-permute-start | bytes 589832 | tf_op jit(solution)/shard_map/ppermute | solution.py:105
  12.1 1.7 %collective-permute-start.2 = (bf16[2,16,3072]{2,1,0:T(8,128)(2,1)S(1)}, bf16[2,16,3072]{2,1,0:T(8,128)(2,1)}, u32[]{:S(2)}, u32[]{:S(2)}) collective-permute-start(bf16[2,16,3072]{2,1,0:T(8,128)(2,1)S(1)} %get-tuple-element.36), channel_id=1, source_target_pairs={{0,3},{1,2},{2,1},{3,0},{8,11},{9,10},{10,9},{11,8},{16,19},{17,18... | collective-permute-start | bytes 589832 | tf_op jit(solution)/shard_map/ppermute | solution.py:105
  13.5 20.1 %copy-start.5 = (pred[4]{0:T(512)(128)(4,1)}, pred[4]{0:T(512)(128)(4,1)S(1)}, u32[]{:S(2)}) copy-start(pred[4]{0:T(512)(128)(4,1)S(1)} %get-tuple-element.21) | copy-start | bytes 16
  13.5 19.5 %copy-start.8 = (s32[1024]{0:T(1024)}, s32[1024]{0:T(1024)S(1)}, u32[]{:S(2)}) copy-start(s32[1024]{0:T(1024)S(1)} %pad_clamp_fusion.2) | copy-start | bytes 12292
  13.6 21.0 %copy-start.10 = (pred[4]{0:T(512)(128)(4,1)}, pred[4]{0:T(512)(128)(4,1)S(1)}, u32[]{:S(2)}) copy-start(pred[4]{0:T(512)(128)(4,1)S(1)} %get-tuple-element.19) | copy-start | bytes 16
  13.7 20.4 %copy-start.9 = (s32[1024]{0:T(1024)}, s32[1024]{0:T(1024)S(1)}, u32[]{:S(2)}) copy-start(s32[1024]{0:T(1024)S(1)} %pad_clamp_fusion.1) | copy-start | bytes 12292
  13.7 10.5 %collective-permute-start.5 = (bf16[176,768]{1,0:T(8,128)(2,1)}, bf16[176,768]{1,0:T(8,128)(2,1)}, u32[]{:S(2)}, u32[]{:S(2)}) collective-permute-start(bf16[176,768]{1,0:T(8,128)(2,1)} %get-tuple-element.16), channel_id=1, source_target_pairs={{0,24},{8,16},{16,8},{24,0},{1,25},{9,17},{17,9},{25,1},{2,26},{10... | collective-permute-start | bytes 811016 | tf_op jit(solution)/shard_map/ppermute | solution.py:82
  15.2 1.3 %copy-start.1 = (bf16[1,1,3072,176]{2,3,1,0:T(8,128)(2,1)S(1)}, bf16[1,1,3072,176]{2,3,1,0:T(8,128)(2,1)}, u32[]{:S(2)}) copy-start(bf16[1,1,3072,176]{2,3,1,0:T(8,128)(2,1)} %param.14) | copy-start | bytes 3244036
  17.7 15.4 %all-to-all-start = ((bf16[4,128,176]{1,2,0:T(8,128)(2,1)}), bf16[4,128,176]{1,2,0:T(8,128)(2,1)S(1)}, u32[]{:S(2)}, u32[]{:S(2)}) async-start(bf16[4,128,176]{1,2,0:T(8,128)(2,1)} %broadcast_in_dim.85), calls=%async_computation | async-start | bytes 360448 | tf_op jit(solution)/shard_map/all_to_all | solution.py:114
  35.5 7.5 %all-to-all-start.1 = ((bf16[2,4,16,768]{3,2,0,1:T(8,128)(2,1)}), bf16[2,4,16,768]{3,2,0,1:T(8,128)(2,1)S(1)}, u32[]{:S(2)}, u32[]{:S(2)}) async-start(bf16[2,4,16,768]{3,2,0,1:T(8,128)(2,1)} %select_bitcast_fusion.2), calls=%async_computation.1 | async-start | bytes 393216 | tf_op jit(solution)/shard_map/all_to_all | solution.py:127
  38.9 21.1 %copy-start.6 = (pred[4]{0:T(512)(128)(4,1)S(1)}, pred[4]{0:T(512)(128)(4,1)}, u32[]{:S(2)}) copy-start(pred[4]{0:T(512)(128)(4,1)} %copy-done.5) | copy-start | bytes 16
  43.2 9.4 %collective-permute-start.6 = (bf16[2,24,768]{2,1,0:T(8,128)(2,1)S(1)}, bf16[2,24,768]{2,1,0:T(8,128)(2,1)S(1)}, u32[]{:S(2)}, u32[]{:S(2)}) collective-permute-start(bf16[2,24,768]{2,1,0:T(8,128)(2,1)S(1)} %fusion), channel_id=1, source_target_pairs={{0,4},{1,5},{2,6},{3,7},{8,12},{9,13},{10,14},{11,15},{16,20},{17,... | collective-permute-start | bytes 221192 | tf_op jit(solution)/shard_map/ppermute | solution.py:159
  44.5 11.7 %collective-permute-start.7 = (bf16[2,24,768]{2,1,0:T(8,128)(2,1)S(1)}, bf16[2,24,768]{2,1,0:T(8,128)(2,1)S(1)}, u32[]{:S(2)}, u32[]{:S(2)}) collective-permute-start(bf16[2,24,768]{2,1,0:T(8,128)(2,1)S(1)} %fusion), channel_id=1, source_target_pairs={{0,12},{1,13},{2,14},{3,15},{8,4},{9,5},{10,6},{11,7},{16,28},{17,... | collective-permute-start | bytes 221192 | tf_op jit(solution)/shard_map/ppermute | solution.py:159
  45.8 11.3 %collective-permute-start.8 = (bf16[2,24,768]{2,1,0:T(8,128)(2,1)S(1)}, bf16[2,24,768]{2,1,0:T(8,128)(2,1)S(1)}, u32[]{:S(2)}, u32[]{:S(2)}) collective-permute-start(bf16[2,24,768]{2,1,0:T(8,128)(2,1)S(1)} %fusion), channel_id=1, source_target_pairs={{0,20},{1,21},{2,22},{3,23},{8,28},{9,29},{10,30},{11,31},{16,4},{... | collective-permute-start | bytes 221192 | tf_op jit(solution)/shard_map/ppermute | solution.py:159
  47.1 12.3 %collective-permute-start.9 = (bf16[2,24,768]{2,1,0:T(8,128)(2,1)S(1)}, bf16[2,24,768]{2,1,0:T(8,128)(2,1)S(1)}, u32[]{:S(2)}, u32[]{:S(2)}) collective-permute-start(bf16[2,24,768]{2,1,0:T(8,128)(2,1)S(1)} %fusion), channel_id=1, source_target_pairs={{0,28},{1,29},{2,30},{3,31},{8,20},{9,21},{10,22},{11,23},{16,12},... | collective-permute-start | bytes 221192 | tf_op jit(solution)/shard_map/ppermute | solution.py:159
  60.6 8.4 %collective-permute-start.10 = (bf16[2,16,3072]{2,1,0:T(8,128)(2,1)S(1)}, bf16[2,16,3072]{2,1,0:T(8,128)(2,1)S(1)}, u32[]{:S(2)}, u32[]{:S(2)}) collective-permute-start(bf16[2,16,3072]{2,1,0:T(8,128)(2,1)S(1)} %get-tuple-element.31), channel_id=1, source_target_pairs={{4,5},{5,4},{6,7},{7,6},{12,13},{13,12},{14,15},{15,14},{20,21},{2... | collective-permute-start | bytes 589832 | tf_op jit(solution)/shard_map/ppermute | solution.py:105
  63.3 6.7 %collective-permute-start.11 = (bf16[2,16,3072]{2,1,0:T(8,128)(2,1)S(1)}, bf16[2,16,3072]{2,1,0:T(8,128)(2,1)S(1)}, u32[]{:S(2)}, u32[]{:S(2)}) collective-permute-start(bf16[2,16,3072]{2,1,0:T(8,128)(2,1)S(1)} %get-tuple-element.30), channel_id=1, source_target_pairs={{4,6},{5,7},{6,4},{7,5},{12,14},{13,15},{14,12},{15,13},{20,22},{2... | collective-permute-start | bytes 589832 | tf_op jit(solution)/shard_map/ppermute | solution.py:105
  65.5 7.5 %collective-permute-start.12 = (bf16[2,16,3072]{2,1,0:T(8,128)(2,1)S(1)}, bf16[2,16,3072]{2,1,0:T(8,128)(2,1)S(1)}, u32[]{:S(2)}, u32[]{:S(2)}) collective-permute-start(bf16[2,16,3072]{2,1,0:T(8,128)(2,1)S(1)} %get-tuple-element.32), channel_id=1, source_target_pairs={{4,7},{5,6},{6,5},{7,4},{12,15},{13,14},{14,13},{15,12},{20,23},{2... | collective-permute-start | bytes 589832 | tf_op jit(solution)/shard_map/ppermute | solution.py:105
  73.3 1.3 %copy-start.2 = (bf16[1,1,3072,176]{2,3,1,0:T(8,128)(2,1)S(1)}, bf16[1,1,3072,176]{2,3,1,0:T(8,128)(2,1)}, u32[]{:S(2)}) copy-start(bf16[1,1,3072,176]{2,3,1,0:T(8,128)(2,1)} %param.14) | copy-start | bytes 3244036
  74.6 9.6 %copy-start.7 = (pred[4]{0:T(512)(128)(4,1)S(1)}, pred[4]{0:T(512)(128)(4,1)}, u32[]{:S(2)}) copy-start(pred[4]{0:T(512)(128)(4,1)} %copy-done.5) | copy-start | bytes 16
  84.1 1.1 %copy-start.11 = (pred[4]{0:T(512)(128)(4,1)S(1)}, pred[4]{0:T(512)(128)(4,1)}, u32[]{:S(2)}) copy-start(pred[4]{0:T(512)(128)(4,1)} %copy-done.10) | copy-start | bytes 16
  86.1 7.4 %all-to-all-start.3 = ((bf16[2,4,16,768]{3,2,0,1:T(8,128)(2,1)}), bf16[2,4,16,768]{3,2,0,1:T(8,128)(2,1)S(1)}, u32[]{:S(2)}, u32[]{:S(2)}) async-start(bf16[2,4,16,768]{3,2,0,1:T(8,128)(2,1)} %select_bitcast_fusion.1), calls=%async_computation.3 | async-start | bytes 393216 | tf_op jit(solution)/shard_map/all_to_all | solution.py:127
where the time goes:
time: 95.2 us; the launch traced here: 94.3 us
  starting transfers between devices  33.4 us (35%)
  waiting for transfers between devices  30.7 us (32%)
  local copies, waits for them, and re-layouts  12.3 us (13%)
  blocking collectives  8.35 us (9%)
  other arithmetic  4.58 us (5%)
  matrix products  4.44 us (5%)
    ppermute x6, starting transfers between devices, layer(): lax.ppermute(outgoing[:, s], AXES, expert_pairs(p, s, False))  12.4 us
    ppermute x4, waiting for transfers between devices, per_device(): parts.append(lax.ppermute(cols, AXES, pairs))  11 us
    all_to_all x1, blocking collectives, layer(): gathered = lax.all_to_all(spread, 'dp', 0, 0, tiled=True)  8.35 us
    all_to_all x1, waiting for transfers between devices, layer(): gathered = lax.all_to_all(spread, 'dp', 0, 0, tiled=True)  7.92 us
    all_to_all x2, waiting for transfers between devices, layer(): lax.all_to_all(by_block, 'expert', 1, 1, tiled=True)  7.88 us
    all_to_all x2, starting transfers between devices, layer(): lax.all_to_all(by_block, 'expert', 1, 1, tiled=True)  6.8 us
    ppermute x4, starting transfers between devices, per_device(): parts.append(lax.ppermute(cols, AXES, pairs))  5.17 us
    all_to_all x1, starting transfers between devices, layer(): gathered = lax.all_to_all(spread, 'dp', 0, 0, tiled=True)  4.51 us
  transfers between devices with their start and end apart: 16, of which 9 were waited for; matrix products, arithmetic and copies ran while one was open for 10% of the time, Pallas kernels for 0%

commit v1 on v0

--- a/solution.py
+++ b/solution.py
@@ -1,3 +1,4 @@
+import functools
 import jax
 import jax.numpy as jnp
 from jax import lax
@@ -7,6 +8,22 @@
 CAP = 16
 AXES = ("dp", "pipe", "expert")
 SMALL_GROUP = 8
+
+
+def raise_routes_all_all(vals, where_dim, d_out):
+    main = jnp.concatenate(
+        jax.lax.all_to_all(
+            jnp.stack(jnp.split(vals, jax.lax.axis_size("expert"), axis=where_dim), axis=0),
+            "expert",
+            0,
+            0,
+        ),
+        axis=d_out,
+    )
+    return main
+
+
+knots_update = functools.partial(raise_routes_all_all, where_dim=1, d_out=1)
 
 
 class Ring:
@@ -124,9 +141,7 @@
         if ering.xor:
             order = jnp.stack([ering.place(j, e_me) for j in range(n_exp)])
             by_block = jnp.take(expert_out, order, axis=1)
-            returned = lax.all_to_all(by_block, "expert", 1, 1, tiled=True).reshape(
-                micro, rows_all, columns
-            )
+            returned = knots_update(by_block).reshape(micro, rows_all, columns)
         else:
             returned = [expert_out[:, 0]]
             for s in range(1, n_exp):

time: 95.2 us -> 95.3 us (level)
    another operation x0 -> x2, other arithmetic: none -> 1.41 us  [raise_routes_all_all(): jnp.stack(jnp.split(vals, jax.lax.axis_size('expert'), axis=where_dim), a...]
    select_n x2, other arithmetic: 1.55 us -> 0.18 us  [layer(): by_block = jnp.take(expert_out, order, axis=1)]
where the time goes in v1:
time: 95.3 us; the launch traced here: 94.4 us
  starting transfers between devices  33.3 us (35%)
  waiting for transfers between devices  30.8 us (32%)
  local copies, waits for them, and re-layouts  12.4 us (13%)
  blocking collectives  8.35 us (9%)
  other arithmetic  4.62 us (5%)
  matrix products  4.43 us (5%)
    ppermute x6, starting transfers between devices, layer(): lax.ppermute(outgoing[:, s], AXES, expert_pairs(p, s, False))  12.4 us
    ppermute x4, waiting for transfers between devices, per_device(): parts.append(lax.ppermute(cols, AXES, pairs))  11 us
    all_to_all x1, blocking collectives, layer(): gathered = lax.all_to_all(spread, 'dp', 0, 0, tiled=True)  8.35 us
    all_to_all x1, waiting for transfers between devices, layer(): gathered = lax.all_to_all(spread, 'dp', 0, 0, tiled=True)  7.95 us
    all_to_all x2, waiting for transfers between devices, raise_routes_all_all(): jax.lax.all_to_all(jnp.stack(jnp.split(vals, jax.lax.axis_size('expert'),...  7.88 us
    all_to_all x2, starting transfers between devices, raise_routes_all_all(): jax.lax.all_to_all(jnp.stack(jnp.split(vals, jax.lax.axis_size('expert'),...  6.8 us
    ppermute x4, starting transfers between devices, per_device(): parts.append(lax.ppermute(cols, AXES, pairs))  5.17 us
    ppermute x3, starting transfers between devices, per_device(): lax.ppermute(down_parts[s], 'dp', [(i, dring.ahead(i, s)) for i in range(...  4.51 us
  transfers between devices with their start and end apart: 16, of which 9 were waited for; matrix products, arithmetic and copies ran while one was open for 10% of the time, Pallas kernels for 0%

profile of v1, /device:TPU:1, one launch (start us, length us, event | category | flops | bytes accessed | tf_op | source)
XLA Modules:
  0.0 94.4 jit_solution(10729555722182896590)
XLA Ops:
  0.0 2.2 %dynamic-slice_bitcast_fusion = (bf16[176,768]{1,0:T(8,128)(2,1)}, bf16[176,768]{1,0:T(8,128)(2,1)}, bf16[176,768]{1,0:T(8,128)(2,1)S(1)}, bf16[176,768]{1,0:T(8,128)(2,1)}) fusion(bf16[1,1,176,3072]{3,2,1,0:T(8,128)(2,1)} %param.15, s32[]{:T(128)S(6)} %select_n.72, s32[]{:T(128)S(6)} %select_n.70, s32[]{:T(128)S(6)} %select_n.69, s32[]{:T(128)S(6)} %select_n.71), kind=kLoop, calls=%fused_computation.33 | loop fusion | bytes 2162704 | tf_op jit(solution)/shard_map/dynamic_slice | solution.py:95
  2.2 2.1 %collective-permute-start.3 = (bf16[176,768]{1,0:T(8,128)(2,1)}, bf16[176,768]{1,0:T(8,128)(2,1)}, u32[]{:S(2)}, u32[]{:S(2)}) collective-permute-start(bf16[176,768]{1,0:T(8,128)(2,1)} %get-tuple-element.14), channel_id=1, source_target_pairs={{0,8},{8,0},{16,24},{24,16},{1,9},{9,1},{17,25},{25,17},{2,10},{10... | collective-permute-start | bytes 811016 | tf_op jit(solution)/shard_map/ppermute | solution.py:99
  4.4 2.3 %collective-permute-start.4 = (bf16[176,768]{1,0:T(8,128)(2,1)}, bf16[176,768]{1,0:T(8,128)(2,1)}, u32[]{:S(2)}, u32[]{:S(2)}) collective-permute-start(bf16[176,768]{1,0:T(8,128)(2,1)} %get-tuple-element.15), channel_id=1, source_target_pairs={{0,16},{8,24},{16,0},{24,8},{1,17},{9,25},{17,1},{25,9},{2,18},{10... | collective-permute-start | bytes 811016 | tf_op jit(solution)/shard_map/ppermute | solution.py:99
  6.7 0.1 copy.85
  6.8 0.1 eq.48
  7.0 0.2 select_reduce_fusion.3
  7.2 0.1 reduce_sum.85
  7.5 0.1 eq.55
  7.7 0.2 select_reduce_fusion.1
  7.9 0.1 reduce_sum.88
  8.1 0.1 convert_reduce_fusion
  8.2 0.4 convolution_convert_fusion.1
  8.7 0.7 fusion.20
  9.4 1.3 %collective-permute-start = (bf16[2,16,3072]{2,1,0:T(8,128)(2,1)}, bf16[2,16,3072]{2,1,0:T(8,128)(2,1)}, u32[]{:S(2)}, u32[]{:S(2)}) collective-permute-start(bf16[2,16,3072]{2,1,0:T(8,128)(2,1)} %get-tuple-element.35), channel_id=1, source_target_pairs={{0,1},{1,0},{2,3},{3,2},{8,9},{9,8},{10,11},{11,10},{16,17},{17,16... | collective-permute-start | bytes 589832 | tf_op jit(solution)/shard_map/ppermute | solution.py:122
  10.7 1.3 %collective-permute-start.1 = (bf16[2,16,3072]{2,1,0:T(8,128)(2,1)S(1)}, bf16[2,16,3072]{2,1,0:T(8,128)(2,1)}, u32[]{:S(2)}, u32[]{:S(2)}) collective-permute-start(bf16[2,16,3072]{2,1,0:T(8,128)(2,1)S(1)} %get-tuple-element.34), channel_id=1, source_target_pairs={{0,2},{1,3},{2,0},{3,1},{8,10},{9,11},{10,8},{11,9},{16,18},{17,19... | collective-permute-start | bytes 589832 | tf_op jit(solution)/shard_map/ppermute | solution.py:122
  12.1 1.3 %collective-permute-start.2 = (bf16[2,16,3072]{2,1,0:T(8,128)(2,1)S(1)}, bf16[2,16,3072]{2,1,0:T(8,128)(2,1)}, u32[]{:S(2)}, u32[]{:S(2)}) collective-permute-start(bf16[2,16,3072]{2,1,0:T(8,128)(2,1)S(1)} %get-tuple-element.36), channel_id=1, source_target_pairs={{0,3},{1,2},{2,1},{3,0},{8,11},{9,10},{10,9},{11,8},{16,19},{17,18... | collective-permute-start | bytes 589832 | tf_op jit(solution)/shard_map/ppermute | solution.py:122
  13.8 1.3 %multiply_reduce_fusion.1 = (f32[2,4,16]{2,1,0:T(4,128)S(1)}, bf16[2,4,16,3072]{3,2,1,0:T(8,128)(2,1)S(1)}) fusion(bf16[2,1,16,3072]{3,2,1,0:T(8,128)(2,1)} %bitcast.28, bf16[2,1,16,3072]{3,2,1,0:T(8,128)(2,1)} %bitcast.26, bf16[2,1,16,3072]{3,2,1,0:T(8,128)(2,1)} %bitcast.24, bf16[2,1,16,3072]{3,2,1,0:T(8,128)(2,1)S(1)} %get-tuple-element.33), kind=kLoop, calls=%fused_computation.8 | loop fusion | flops 2359168 | bytes 1573376 | tf_op jit(solution)/shard_map/reduce_sum | solution.py:124
  15.2 0.4 convolution_multiply_fusion.3
  15.7 0.8 copy-done.1
  16.5 0.5 fusion.6
  17.0 0.7 broadcast_in_dim.85
  17.6 4.5 %all-to-all-start = ((bf16[4,128,176]{1,2,0:T(8,128)(2,1)}), bf16[4,128,176]{1,2,0:T(8,128)(2,1)S(1)}, u32[]{:S(2)}, u32[]{:S(2)}) async-start(bf16[4,128,176]{1,2,0:T(8,128)(2,1)} %broadcast_in_dim.85), calls=%async_computation | async-start | bytes 360448 | tf_op jit(solution)/shard_map/all_to_all | solution.py:131
  22.1 1.0 %constant_dynamic-update-slice_fusion.2 = bf16[704,768]{1,0:T(8,128)(2,1)S(1)} fusion(bf16[704,768]{1,0:T(8,128)(2,1)S(1)} %constant_dynamic-update-slice_fusion.3, bf16[176,768]{1,0:T(8,128)(2,1)} %collective-permute-done.3), kind=kLoop, calls=%fused_computation.75 | loop fusion | bytes 540672
  23.1 1.0 %constant_dynamic-update-slice_fusion.1 = bf16[704,768]{1,0:T(8,128)(2,1)S(1)} fusion(bf16[704,768]{1,0:T(8,128)(2,1)S(1)} %constant_dynamic-update-slice_fusion.2, bf16[176,768]{1,0:T(8,128)(2,1)} %collective-permute-done.4), kind=kLoop, calls=%fused_computation.74 | loop fusion | bytes 540672
  24.1 1.0 %constant_dynamic-update-slice_fusion = bf16[704,768]{1,0:T(8,128)(2,1)S(1)} fusion(bf16[704,768]{1,0:T(8,128)(2,1)S(1)} %constant_dynamic-update-slice_fusion.1, bf16[176,768]{1,0:T(8,128)(2,1)} %collective-permute-done.5), kind=kLoop, calls=%fused_computation.73 | loop fusion | bytes 540672 | tf_op jit(solution)/shard_map/concatenate | solution.py:102
  25.1 7.9 %all-to-all-done = bf16[4,128,176]{1,2,0:T(8,128)(2,1)S(1)} async-done(((bf16[4,128,176]{1,2,0:T(8,128)(2,1)}), bf16[4,128,176]{1,2,0:T(8,128)(2,1)S(1)}, u32[]{:S(2)}, u32[]{:S(2)}) %all-to-all-start) | async-done | bytes 180256 | tf_op jit(solution)/shard_map/all_to_all | solution.py:131
  33.0 0.6 gather_fusion.1
  33.7 0.4 convolution_convert_fusion.3
  34.1 0.6 gather_fusion.2
  34.7 0.1 select_bitcast_fusion.2
  34.8 0.7 pad_maximum_fusion.3
  35.5 3.4 %all-to-all-start.1 = ((bf16[4,2,1,16,768]{4,3,1,2,0:T(8,128)(2,1)}), bf16[4,2,1,16,768]{4,3,1,2,0:T(8,128)(2,1)S(1)}, u32[]{:S(2)}, u32[]{:S(2)}) async-start(bf16[4,2,1,16,768]{4,3,1,2,0:T(8,128)(2,1)} %pad_maximum_fusion.3), calls=%async_computation.1 | async-start | bytes 393216 | tf_op jit(solution)/shard_map/all_to_all | solution.py:15
  39.0 0.1 select_reduce_fusion
  39.1 3.9 %all-to-all-done.1 = bf16[4,2,1,16,768]{4,3,1,2,0:T(8,128)(2,1)S(1)} async-done(((bf16[4,2,1,16,768]{4,3,1,2,0:T(8,128)(2,1)}), bf16[4,2,1,16,768]{4,3,1,2,0:T(8,128)(2,1)S(1)}, u32[]{:S(2)}, u32[]{:S(2)}) %all-to-all-start.1) | async-done | bytes 196640 | tf_op jit(solution)/shard_map/all_to_all | solution.py:15
  43.0 0.2 fusion
  43.2 1.3 %collective-permute-start.6 = (bf16[2,24,768]{2,1,0:T(8,128)(2,1)S(1)}, bf16[2,24,768]{2,1,0:T(8,128)(2,1)S(1)}, u32[]{:S(2)}, u32[]{:S(2)}) collective-permute-start(bf16[2,24,768]{2,1,0:T(8,128)(2,1)S(1)} %fusion), channel_id=1, source_target_pairs={{0,4},{1,5},{2,6},{3,7},{8,12},{9,13},{10,14},{11,15},{16,20},{17,... | collective-permute-start | bytes 221192 | tf_op jit(solution)/shard_map/ppermute | solution.py:174
  44.5 1.3 %collective-permute-start.7 = (bf16[2,24,768]{2,1,0:T(8,128)(2,1)S(1)}, bf16[2,24,768]{2,1,0:T(8,128)(2,1)S(1)}, u32[]{:S(2)}, u32[]{:S(2)}) collective-permute-start(bf16[2,24,768]{2,1,0:T(8,128)(2,1)S(1)} %fusion), channel_id=1, source_target_pairs={{0,12},{1,13},{2,14},{3,15},{8,4},{9,5},{10,6},{11,7},{16,28},{17,... | collective-permute-start | bytes 221192 | tf_op jit(solution)/shard_map/ppermute | solution.py:174
  45.8 1.3 %collective-permute-start.8 = (bf16[2,24,768]{2,1,0:T(8,128)(2,1)S(1)}, bf16[2,24,768]{2,1,0:T(8,128)(2,1)S(1)}, u32[]{:S(2)}, u32[]{:S(2)}) collective-permute-start(bf16[2,24,768]{2,1,0:T(8,128)(2,1)S(1)} %fusion), channel_id=1, source_target_pairs={{0,20},{1,21},{2,22},{3,23},{8,28},{9,29},{10,30},{11,31},{16,4},{... | collective-permute-start | bytes 221192 | tf_op jit(solution)/shard_map/ppermute | solution.py:174
  47.1 1.3 %collective-permute-start.9 = (bf16[2,24,768]{2,1,0:T(8,128)(2,1)S(1)}, bf16[2,24,768]{2,1,0:T(8,128)(2,1)S(1)}, u32[]{:S(2)}, u32[]{:S(2)}) collective-permute-start(bf16[2,24,768]{2,1,0:T(8,128)(2,1)S(1)} %fusion), channel_id=1, source_target_pairs={{0,28},{1,29},{2,30},{3,31},{8,20},{9,21},{10,22},{11,23},{16,12},... | collective-permute-start | bytes 221192 | tf_op jit(solution)/shard_map/ppermute | solution.py:174
  48.4 4.2 %collective-permute-done.6 = bf16[2,24,768]{2,1,0:T(8,128)(2,1)S(1)} collective-permute-done((bf16[2,24,768]{2,1,0:T(8,128)(2,1)S(1)}, bf16[2,24,768]{2,1,0:T(8,128)(2,1)S(1)}, u32[]{:S(2)}, u32[]{:S(2)}) %collective-permute-start.6) | collective-permute-done | bytes 73760 | tf_op jit(solution)/shard_map/ppermute | solution.py:174
  52.6 3.6 %collective-permute-done.7 = bf16[2,24,768]{2,1,0:T(8,128)(2,1)S(1)} collective-permute-done((bf16[2,24,768]{2,1,0:T(8,128)(2,1)S(1)}, bf16[2,24,768]{2,1,0:T(8,128)(2,1)S(1)}, u32[]{:S(2)}, u32[]{:S(2)}) %collective-permute-start.7) | collective-permute-done | bytes 73760 | tf_op jit(solution)/shard_map/ppermute | solution.py:174
  56.3 0.8 collective-permute-done.8
  57.1 2.3 %collective-permute-done.9 = bf16[2,24,768]{2,1,0:T(8,128)(2,1)S(1)} collective-permute-done((bf16[2,24,768]{2,1,0:T(8,128)(2,1)S(1)}, bf16[2,24,768]{2,1,0:T(8,128)(2,1)S(1)}, u32[]{:S(2)}, u32[]{:S(2)}) %collective-permute-start.9) | collective-permute-done | bytes 73760 | tf_op jit(solution)/shard_map/ppermute | solution.py:174
  59.4 0.6 gather_fusion
  60.0 0.1 select_bitcast_fusion
  60.1 0.4 convolution_convert_fusion
  60.6 2.7 %collective-permute-start.10 = (bf16[2,16,3072]{2,1,0:T(8,128)(2,1)S(1)}, bf16[2,16,3072]{2,1,0:T(8,128)(2,1)S(1)}, u32[]{:S(2)}, u32[]{:S(2)}) collective-permute-start(bf16[2,16,3072]{2,1,0:T(8,128)(2,1)S(1)} %get-tuple-element.31), channel_id=1, source_target_pairs={{4,5},{5,4},{6,7},{7,6},{12,13},{13,12},{14,15},{15,14},{20,21},{2... | collective-permute-start | bytes 589832 | tf_op jit(solution)/shard_map/ppermute | solution.py:122
  63.4 2.2 %collective-permute-start.11 = (bf16[2,16,3072]{2,1,0:T(8,128)(2,1)S(1)}, bf16[2,16,3072]{2,1,0:T(8,128)(2,1)S(1)}, u32[]{:S(2)}, u32[]{:S(2)}) collective-permute-start(bf16[2,16,3072]{2,1,0:T(8,128)(2,1)S(1)} %get-tuple-element.30), channel_id=1, source_target_pairs={{4,6},{5,7},{6,4},{7,5},{12,14},{13,15},{14,12},{15,13},{20,22},{2... | collective-permute-start | bytes 589832 | tf_op jit(solution)/shard_map/ppermute | solution.py:122
  65.5 3.5 %collective-permute-start.12 = (bf16[2,16,3072]{2,1,0:T(8,128)(2,1)S(1)}, bf16[2,16,3072]{2,1,0:T(8,128)(2,1)S(1)}, u32[]{:S(2)}, u32[]{:S(2)}) collective-permute-start(bf16[2,16,3072]{2,1,0:T(8,128)(2,1)S(1)} %get-tuple-element.32), channel_id=1, source_target_pairs={{4,7},{5,6},{6,5},{7,4},{12,15},{13,14},{14,13},{15,12},{20,23},{2... | collective-permute-start | bytes 589832 | tf_op jit(solution)/shard_map/ppermute | solution.py:122
  69.0 1.0 %collective-permute-done.11 = bf16[2,16,3072]{2,1,0:T(8,128)(2,1)S(1)} collective-permute-done((bf16[2,16,3072]{2,1,0:T(8,128)(2,1)S(1)}, bf16[2,16,3072]{2,1,0:T(8,128)(2,1)S(1)}, u32[]{:S(2)}, u32[]{:S(2)}) %collective-permute-start.11) | collective-permute-done | bytes 196640 | tf_op jit(solution)/shard_map/ppermute | solution.py:122
  70.1 2.9 %collective-permute-done.12 = bf16[2,16,3072]{2,1,0:T(8,128)(2,1)S(1)} collective-permute-done((bf16[2,16,3072]{2,1,0:T(8,128)(2,1)S(1)}, bf16[2,16,3072]{2,1,0:T(8,128)(2,1)S(1)}, u32[]{:S(2)}, u32[]{:S(2)}) %collective-permute-start.12) | collective-permute-done | bytes 196640 | tf_op jit(solution)/shard_map/ppermute | solution.py:122
  73.0 0.2 multiply_reduce_fusion
  73.3 0.1 rsqrt.25
  73.4 0.5 convolution_multiply_fusion.1
  73.8 0.8 copy-done.2
  74.6 0.5 fusion.7
  75.1 8.3 %all_to_all.20 = bf16[4,128,176]{1,2,0:T(8,128)(2,1)S(1)} all-to-all(bf16[4,128,176]{1,2,0:T(8,128)(2,1)S(1)} %broadcast_in_dim.87), channel_id=1, replica_groups=mesh['dp'=4,'pipe'=2,'expert'=4] {'dp'}, dimensions={0} | all-to-all | bytes 360448 | tf_op jit(solution)/shard_map/all_to_all | solution.py:131
  83.5 0.7 gather_fusion.3
  84.3 0.3 convolution_convert_fusion.2
  84.6 0.7 gather_fusion.4
  85.5 0.7 pad_maximum_fusion.4
  86.2 3.4 %all-to-all-start.3 = ((bf16[4,2,1,16,768]{4,3,1,2,0:T(8,128)(2,1)}), bf16[4,2,1,16,768]{4,3,1,2,0:T(8,128)(2,1)S(1)}, u32[]{:S(2)}, u32[]{:S(2)}) async-start(bf16[4,2,1,16,768]{4,3,1,2,0:T(8,128)(2,1)} %pad_maximum_fusion.4), calls=%async_computation.3 | async-start | bytes 393216 | tf_op jit(solution)/shard_map/all_to_all | solution.py:15
  89.5 4.0 %all-to-all-done.3 = bf16[4,2,1,16,768]{4,3,1,2,0:T(8,128)(2,1)S(1)} async-done(((bf16[4,2,1,16,768]{4,3,1,2,0:T(8,128)(2,1)}), bf16[4,2,1,16,768]{4,3,1,2,0:T(8,128)(2,1)S(1)}, u32[]{:S(2)}, u32[]{:S(2)}) %all-to-all-start.3) | async-done | bytes 196640 | tf_op jit(solution)/shard_map/all_to_all | solution.py:15
  93.6 0.9 fusion.5
  (63 shorter events, 1.6 us)
Async XLA Ops:
  0.0 15.2 %copy-start = (bf16[1,1,3072,176]{2,3,1,0:T(8,128)(2,1)S(1)}, bf16[1,1,3072,176]{2,3,1,0:T(8,128)(2,1)}, u32[]{:S(2)}) copy-start(bf16[1,1,3072,176]{2,3,1,0:T(8,128)(2,1)} %param.13) | copy-start | bytes 3244036
  0.0 6.7 %copy-start.4 = (s32[1,2,24,2]{2,3,1,0:T(2,128)S(1)}, s32[1,2,24,2]{2,3,1,0:T(2,128)}, u32[]{:S(2)}) copy-start(s32[1,2,24,2]{2,3,1,0:T(2,128)} %param.11) | copy-start | bytes 1156
  0.0 8.2 %copy-start.3 = (bf16[2,24,3072]{2,1,0:T(8,128)(2,1)S(1)}, bf16[2,24,3072]{2,1,0:T(8,128)(2,1)}, u32[]{:S(2)}) copy-start(bf16[2,24,3072]{2,1,0:T(8,128)(2,1)} %param.10) | copy-start | bytes 884740
  2.2 19.9 %collective-permute-start.3 = (bf16[176,768]{1,0:T(8,128)(2,1)}, bf16[176,768]{1,0:T(8,128)(2,1)}, u32[]{:S(2)}, u32[]{:S(2)}) collective-permute-start(bf16[176,768]{1,0:T(8,128)(2,1)} %get-tuple-element.14), channel_id=1, source_target_pairs={{0,8},{8,0},{16,24},{24,16},{1,9},{9,1},{17,25},{25,17},{2,10},{10... | collective-permute-start | bytes 811016 | tf_op jit(solution)/shard_map/ppermute | solution.py:99
  4.4 18.8 %collective-permute-start.4 = (bf16[176,768]{1,0:T(8,128)(2,1)}, bf16[176,768]{1,0:T(8,128)(2,1)}, u32[]{:S(2)}, u32[]{:S(2)}) collective-permute-start(bf16[176,768]{1,0:T(8,128)(2,1)} %get-tuple-element.15), channel_id=1, source_target_pairs={{0,16},{8,24},{16,0},{24,8},{1,17},{9,25},{17,1},{25,9},{2,18},{10... | collective-permute-start | bytes 811016 | tf_op jit(solution)/shard_map/ppermute | solution.py:99
  8.6 5.0 %copy-start.12 = (f32[1,2,24,2]{2,3,1,0:T(2,128)S(1)}, f32[1,2,24,2]{2,3,1,0:T(2,128)}, u32[]{:S(2)}) copy-start(f32[1,2,24,2]{2,3,1,0:T(2,128)} %param.12) | copy-start | bytes 1156
  9.4 4.3 %collective-permute-start = (bf16[2,16,3072]{2,1,0:T(8,128)(2,1)}, bf16[2,16,3072]{2,1,0:T(8,128)(2,1)}, u32[]{:S(2)}, u32[]{:S(2)}) collective-permute-start(bf16[2,16,3072]{2,1,0:T(8,128)(2,1)} %get-tuple-element.35), channel_id=1, source_target_pairs={{0,1},{1,0},{2,3},{3,2},{8,9},{9,8},{10,11},{11,10},{16,17},{17,16... | collective-permute-start | bytes 589832 | tf_op jit(solution)/shard_map/ppermute | solution.py:122
  10.7 3.0 %collective-permute-start.1 = (bf16[2,16,3072]{2,1,0:T(8,128)(2,1)S(1)}, bf16[2,16,3072]{2,1,0:T(8,128)(2,1)}, u32[]{:S(2)}, u32[]{:S(2)}) collective-permute-start(bf16[2,16,3072]{2,1,0:T(8,128)(2,1)S(1)} %get-tuple-element.34), channel_id=1, source_target_pairs={{0,2},{1,3},{2,0},{3,1},{8,10},{9,11},{10,8},{11,9},{16,18},{17,19... | collective-permute-start | bytes 589832 | tf_op jit(solution)/shard_map/ppermute | solution.py:122
  12.1 1.7 %collective-permute-start.2 = (bf16[2,16,3072]{2,1,0:T(8,128)(2,1)S(1)}, bf16[2,16,3072]{2,1,0:T(8,128)(2,1)}, u32[]{:S(2)}, u32[]{:S(2)}) collective-permute-start(bf16[2,16,3072]{2,1,0:T(8,128)(2,1)S(1)} %get-tuple-element.36), channel_id=1, source_target_pairs={{0,3},{1,2},{2,1},{3,0},{8,11},{9,10},{10,9},{11,8},{16,19},{17,18... | collective-permute-start | bytes 589832 | tf_op jit(solution)/shard_map/ppermute | solution.py:122
  13.5 20.1 %copy-start.5 = (pred[4]{0:T(512)(128)(4,1)}, pred[4]{0:T(512)(128)(4,1)S(1)}, u32[]{:S(2)}) copy-start(pred[4]{0:T(512)(128)(4,1)S(1)} %get-tuple-element.21) | copy-start | bytes 16
  13.5 19.5 %copy-start.8 = (s32[1024]{0:T(1024)}, s32[1024]{0:T(1024)S(1)}, u32[]{:S(2)}) copy-start(s32[1024]{0:T(1024)S(1)} %pad_clamp_fusion.2) | copy-start | bytes 12292
  13.6 21.1 %copy-start.10 = (pred[4]{0:T(512)(128)(4,1)}, pred[4]{0:T(512)(128)(4,1)S(1)}, u32[]{:S(2)}) copy-start(pred[4]{0:T(512)(128)(4,1)S(1)} %get-tuple-element.19) | copy-start | bytes 16
  13.6 20.5 %copy-start.9 = (s32[1024]{0:T(1024)}, s32[1024]{0:T(1024)S(1)}, u32[]{:S(2)}) copy-start(s32[1024]{0:T(1024)S(1)} %pad_clamp_fusion.1) | copy-start | bytes 12292
  13.7 10.4 %collective-permute-start.5 = (bf16[176,768]{1,0:T(8,128)(2,1)}, bf16[176,768]{1,0:T(8,128)(2,1)}, u32[]{:S(2)}, u32[]{:S(2)}) collective-permute-start(bf16[176,768]{1,0:T(8,128)(2,1)} %get-tuple-element.16), channel_id=1, source_target_pairs={{0,24},{8,16},{16,8},{24,0},{1,25},{9,17},{17,9},{25,1},{2,26},{10... | collective-permute-start | bytes 811016 | tf_op jit(solution)/shard_map/ppermute | solution.py:99
  15.2 1.3 %copy-start.1 = (bf16[1,1,3072,176]{2,3,1,0:T(8,128)(2,1)S(1)}, bf16[1,1,3072,176]{2,3,1,0:T(8,128)(2,1)}, u32[]{:S(2)}) copy-start(bf16[1,1,3072,176]{2,3,1,0:T(8,128)(2,1)} %param.14) | copy-start | bytes 3244036
  17.6 15.4 %all-to-all-start = ((bf16[4,128,176]{1,2,0:T(8,128)(2,1)}), bf16[4,128,176]{1,2,0:T(8,128)(2,1)S(1)}, u32[]{:S(2)}, u32[]{:S(2)}) async-start(bf16[4,128,176]{1,2,0:T(8,128)(2,1)} %broadcast_in_dim.85), calls=%async_computation | async-start | bytes 360448 | tf_op jit(solution)/shard_map/all_to_all | solution.py:131
  35.5 7.5 %all-to-all-start.1 = ((bf16[4,2,1,16,768]{4,3,1,2,0:T(8,128)(2,1)}), bf16[4,2,1,16,768]{4,3,1,2,0:T(8,128)(2,1)S(1)}, u32[]{:S(2)}, u32[]{:S(2)}) async-start(bf16[4,2,1,16,768]{4,3,1,2,0:T(8,128)(2,1)} %pad_maximum_fusion.3), calls=%async_computation.1 | async-start | bytes 393216 | tf_op jit(solution)/shard_map/all_to_all | solution.py:15
  38.9 21.1 %copy-start.6 = (pred[4]{0:T(512)(128)(4,1)S(1)}, pred[4]{0:T(512)(128)(4,1)}, u32[]{:S(2)}) copy-start(pred[4]{0:T(512)(128)(4,1)} %copy-done.5) | copy-start | bytes 16
  43.2 9.4 %collective-permute-start.6 = (bf16[2,24,768]{2,1,0:T(8,128)(2,1)S(1)}, bf16[2,24,768]{2,1,0:T(8,128)(2,1)S(1)}, u32[]{:S(2)}, u32[]{:S(2)}) collective-permute-start(bf16[2,24,768]{2,1,0:T(8,128)(2,1)S(1)} %fusion), channel_id=1, source_target_pairs={{0,4},{1,5},{2,6},{3,7},{8,12},{9,13},{10,14},{11,15},{16,20},{17,... | collective-permute-start | bytes 221192 | tf_op jit(solution)/shard_map/ppermute | solution.py:174
  44.5 11.7 %collective-permute-start.7 = (bf16[2,24,768]{2,1,0:T(8,128)(2,1)S(1)}, bf16[2,24,768]{2,1,0:T(8,128)(2,1)S(1)}, u32[]{:S(2)}, u32[]{:S(2)}) collective-permute-start(bf16[2,24,768]{2,1,0:T(8,128)(2,1)S(1)} %fusion), channel_id=1, source_target_pairs={{0,12},{1,13},{2,14},{3,15},{8,4},{9,5},{10,6},{11,7},{16,28},{17,... | collective-permute-start | bytes 221192 | tf_op jit(solution)/shard_map/ppermute | solution.py:174
  45.8 11.3 %collective-permute-start.8 = (bf16[2,24,768]{2,1,0:T(8,128)(2,1)S(1)}, bf16[2,24,768]{2,1,0:T(8,128)(2,1)S(1)}, u32[]{:S(2)}, u32[]{:S(2)}) collective-permute-start(bf16[2,24,768]{2,1,0:T(8,128)(2,1)S(1)} %fusion), channel_id=1, source_target_pairs={{0,20},{1,21},{2,22},{3,23},{8,28},{9,29},{10,30},{11,31},{16,4},{... | collective-permute-start | bytes 221192 | tf_op jit(solution)/shard_map/ppermute | solution.py:174
  47.1 12.3 %collective-permute-start.9 = (bf16[2,24,768]{2,1,0:T(8,128)(2,1)S(1)}, bf16[2,24,768]{2,1,0:T(8,128)(2,1)S(1)}, u32[]{:S(2)}, u32[]{:S(2)}) collective-permute-start(bf16[2,24,768]{2,1,0:T(8,128)(2,1)S(1)} %fusion), channel_id=1, source_target_pairs={{0,28},{1,29},{2,30},{3,31},{8,20},{9,21},{10,22},{11,23},{16,12},... | collective-permute-start | bytes 221192 | tf_op jit(solution)/shard_map/ppermute | solution.py:174
  60.6 8.4 %collective-permute-start.10 = (bf16[2,16,3072]{2,1,0:T(8,128)(2,1)S(1)}, bf16[2,16,3072]{2,1,0:T(8,128)(2,1)S(1)}, u32[]{:S(2)}, u32[]{:S(2)}) collective-permute-start(bf16[2,16,3072]{2,1,0:T(8,128)(2,1)S(1)} %get-tuple-element.31), channel_id=1, source_target_pairs={{4,5},{5,4},{6,7},{7,6},{12,13},{13,12},{14,15},{15,14},{20,21},{2... | collective-permute-start | bytes 589832 | tf_op jit(solution)/shard_map/ppermute | solution.py:122
  63.4 6.7 %collective-permute-start.11 = (bf16[2,16,3072]{2,1,0:T(8,128)(2,1)S(1)}, bf16[2,16,3072]{2,1,0:T(8,128)(2,1)S(1)}, u32[]{:S(2)}, u32[]{:S(2)}) collective-permute-start(bf16[2,16,3072]{2,1,0:T(8,128)(2,1)S(1)} %get-tuple-element.30), channel_id=1, source_target_pairs={{4,6},{5,7},{6,4},{7,5},{12,14},{13,15},{14,12},{15,13},{20,22},{2... | collective-permute-start | bytes 589832 | tf_op jit(solution)/shard_map/ppermute | solution.py:122
  65.5 7.5 %collective-permute-start.12 = (bf16[2,16,3072]{2,1,0:T(8,128)(2,1)S(1)}, bf16[2,16,3072]{2,1,0:T(8,128)(2,1)S(1)}, u32[]{:S(2)}, u32[]{:S(2)}) collective-permute-start(bf16[2,16,3072]{2,1,0:T(8,128)(2,1)S(1)} %get-tuple-element.32), channel_id=1, source_target_pairs={{4,7},{5,6},{6,5},{7,4},{12,15},{13,14},{14,13},{15,12},{20,23},{2... | collective-permute-start | bytes 589832 | tf_op jit(solution)/shard_map/ppermute | solution.py:122
  73.3 1.3 %copy-start.2 = (bf16[1,1,3072,176]{2,3,1,0:T(8,128)(2,1)S(1)}, bf16[1,1,3072,176]{2,3,1,0:T(8,128)(2,1)}, u32[]{:S(2)}) copy-start(bf16[1,1,3072,176]{2,3,1,0:T(8,128)(2,1)} %param.14) | copy-start | bytes 3244036
  74.6 9.6 %copy-start.7 = (pred[4]{0:T(512)(128)(4,1)S(1)}, pred[4]{0:T(512)(128)(4,1)}, u32[]{:S(2)}) copy-start(pred[4]{0:T(512)(128)(4,1)} %copy-done.5) | copy-start | bytes 16
  84.2 1.1 %copy-start.11 = (pred[4]{0:T(512)(128)(4,1)S(1)}, pred[4]{0:T(512)(128)(4,1)}, u32[]{:S(2)}) copy-start(pred[4]{0:T(512)(128)(4,1)} %copy-done.10) | copy-start | bytes 16
  86.2 7.4 %all-to-all-start.3 = ((bf16[4,2,1,16,768]{4,3,1,2,0:T(8,128)(2,1)}), bf16[4,2,1,16,768]{4,3,1,2,0:T(8,128)(2,1)S(1)}, u32[]{:S(2)}, u32[]{:S(2)}) async-start(bf16[4,2,1,16,768]{4,3,1,2,0:T(8,128)(2,1)} %pad_maximum_fusion.4), calls=%async_computation.3 | async-start | bytes 393216 | tf_op jit(solution)/shard_map/all_to_all | solution.py:15
